TPU v7x, 128 devices: a whole 4x4x4 slice. The times are simulated.
128 devices in a mesh: req: 16 (over y, x), kvh: 8 (over z, core).
Axes of the slice: x: 4, y: 4, z: 4, core: 2. Of those that a mesh axis runs over, the one named last changes fastest.
Arguments:
- states: bfloat16 [128, 2560], P('req', 'kvh'), may hold values from -6 to 6
- attn_gain: bfloat16 [2560], replicated, may hold values from 0.099609375 to 1.8984375
- w_query: bfloat16 [2560, 4096], P(None, 'kvh'), may hold values from -0.125 to 0.125
- w_key: bfloat16 [2560, 1024], P(None, 'kvh'), may hold values from -0.125 to 0.125
- w_value: bfloat16 [2560, 1024], P(None, 'kvh'), may hold values from -0.125 to 0.125
- query_gain: bfloat16 [128], replicated, may hold values from 0.5 to 2
- key_gain: bfloat16 [128], replicated, may hold values from 0.5 to 2
- w_output: bfloat16 [4096, 2560], P('kvh'), may hold values from -0.25 to 0.25
- ffn_gain: bfloat16 [2560], P('kvh'), may hold values from 0.099609375 to 1.8984375
- w_gate: bfloat16 [2560, 9728], P('kvh', 'req'), may hold values from -0.125 to 0.125
- w_up: bfloat16 [2560, 9728], P('kvh', 'req'), may hold values from -0.125 to 0.125
- w_down: bfloat16 [9728, 2560], P('req', 'kvh'), may hold values from -0.0625 to 0.0625
- kv_pool: bfloat16 [1024, 8, 128, 256], P('req', 'kvh'), may hold values from -6 to 6
- lengths: int32 [128], replicated, may hold values from 1 to 1023, as said below
- page_table: int32 [128, 8], P('req'), may hold values from 0 to 63, as said below
- new_order: int32 [128], replicated, may hold values from 0 to 127, as said below
Outputs:
- output: bfloat16 [128, 2560], P('req', 'kvh')
- new_pool: bfloat16 [1024, 8, 128, 256], P('req', 'kvh')
Inputs may be any that keep to these rules, and one draw needn't show every extreme that they name: `lengths`: each request has at least one cached position and room for the new one; some request has exactly 1023. `page_table`: the 8 rows of one device name each of its 64 pool rows exactly once. `new_order`: A permutation of the requests; slot s lies on the device s // 8. The 8 requests of one device go to 8 different devices, and each device receives its 8 requests from 8 different devices.
All inputs are finite; a program needn't handle non-finite values.
Results may differ from a plain program's by a relative error of at most 0.0087.
Values may be sent and summed in bfloat16 or wider, within the bound.
No kernel may reach another device: no remote copies, remote signals or barrier semaphores. Data moves between devices by JAX's collectives and lax.ppermute only.
A program may use at most 128 MiB of HBM per device.

v0:
```python
import math
import jax
import jax.numpy as jnp
from jax import lax
from jax.sharding import PartitionSpec as P

D = 2560
EPSILON = 1e-06


def rms_norm(values, norm_gain):
    mean_sq = jnp.mean(values * values, axis=-1, keepdims=True)
    return values * lax.rsqrt(mean_sq + EPSILON) * norm_gain


def rotary(values, positions):
    half_dim = values.shape[-1] // 2
    frequency = jnp.exp(
        jnp.arange(half_dim, dtype=jnp.float32) * (-2.0 * math.log(1000000.0) / values.shape[-1])
    )
    angles = positions.astype(jnp.float32)[:, None, None] * frequency
    cosine = jnp.cos(angles)
    sine_part = jnp.sin(angles)
    first_half = values[..., :half_dim]
    second_half = values[..., half_dim:]
    return jnp.concatenate(
        [
            first_half * cosine - second_half * sine_part,
            second_half * cosine + first_half * sine_part,
        ],
        axis=-1,
    )


def mask_blocks(blocks, lengths_now, fresh):
    row_count, pages_per, kv_local, page_len, channels = blocks.shape
    positions = (
        jnp.arange(pages_per, dtype=jnp.int32)[:, None] * page_len
        + jnp.arange(page_len, dtype=jnp.int32)[None, :]
    )
    positions = positions[None, :, None, :, None]
    lengths_col = lengths_now[:, None, None, None, None]
    kept = positions < lengths_col
    placed = positions == lengths_col
    return jnp.where(
        kept, blocks, jnp.where(placed, fresh[:, None, :, None, :], jnp.zeros((), jnp.bfloat16))
    )


def attend(query, sequence, lengths_now):
    row_count, kv_local, span_len, channels = sequence.shape
    head_dim = channels // 2
    q_local = query.shape[1]
    group_size = q_local // kv_local
    grouped = query.reshape(row_count, kv_local, group_size, head_dim)
    scores = jnp.einsum(
        "rkgd,rktd->rkgt", grouped, sequence[..., :head_dim], preferred_element_type=jnp.float32
    ) * (1.0 / math.sqrt(head_dim))
    positions = jnp.arange(span_len, dtype=jnp.int32)
    valid = positions[None, None, None, :] <= lengths_now[:, None, None, None]
    scores = jnp.where(valid, scores, -jnp.inf)
    weights = jax.nn.softmax(scores, axis=-1).astype(jnp.bfloat16)
    mixed = jnp.einsum(
        "rkgt,rktd->rkgd", weights, sequence[..., head_dim:], preferred_element_type=jnp.float32
    )
    return mixed.reshape(row_count, q_local * head_dim).astype(jnp.bfloat16)


def per_device(
    states,
    attn_gain,
    w_query,
    w_key,
    w_value,
    query_gain,
    key_gain,
    w_output,
    ffn_gain,
    w_gate,
    w_up,
    w_down,
    kv_pool,
    lengths,
    page_table,
    new_order,
):
    devices_req = lax.axis_size("req")
    my_index = lax.axis_index("req")
    kvh_index = lax.axis_index("kvh")
    row_count = states.shape[0]
    width_local = states.shape[1]
    head_dim = query_gain.shape[0]
    kv_local = w_key.shape[1] // head_dim
    q_local = w_query.shape[1] // head_dim
    pages_per = page_table.shape[1]
    page_len = kv_pool.shape[2]
    channels = 2 * head_dim
    total_rows = new_order.shape[0]
    everyone = jnp.arange(total_rows, dtype=jnp.int32)
    new_position = jnp.zeros((total_rows,), jnp.int32).at[new_order].set(everyone)
    home = my_index * row_count + jnp.arange(row_count, dtype=jnp.int32)
    destination = new_position[home] // row_count
    peer_ids = jnp.arange(devices_req, dtype=jnp.int32)
    matches = destination[None, :] == peer_ids[:, None]
    picked = jnp.argmax(matches.astype(jnp.int32), axis=1)
    parcels = kv_pool[page_table[picked]]
    received = lax.all_to_all(parcels, "req", split_axis=0, concat_axis=0, tiled=True)
    arriving = lax.dynamic_slice_in_dim(new_order, my_index * row_count, row_count)
    source_owner = arriving // row_count
    full_states = lax.all_gather(states, "kvh", axis=1, tiled=True)
    normed = rms_norm(full_states.astype(jnp.float32), attn_gain.astype(jnp.float32)).astype(
        jnp.bfloat16
    )
    query = jnp.dot(normed, w_query, preferred_element_type=jnp.float32).reshape(
        row_count, q_local, head_dim
    )
    key_new = jnp.dot(normed, w_key, preferred_element_type=jnp.float32).reshape(
        row_count, kv_local, head_dim
    )
    value_new = jnp.dot(normed, w_value, preferred_element_type=jnp.float32).reshape(
        row_count, kv_local, head_dim
    )
    positions_home = lengths[home]
    query = rotary(rms_norm(query, query_gain.astype(jnp.float32)), positions_home).astype(
        jnp.bfloat16
    )
    key_new = rotary(rms_norm(key_new, key_gain.astype(jnp.float32)), positions_home).astype(
        jnp.bfloat16
    )
    fresh = jnp.concatenate([key_new, value_new.astype(jnp.bfloat16)], axis=-1)
    home_blocks = mask_blocks(kv_pool[page_table], positions_home, fresh)
    sequence = home_blocks.transpose(0, 2, 1, 3, 4).reshape(
        row_count, kv_local, pages_per * page_len, channels
    )
    mixed = attend(query, sequence, positions_home)
    partial_out = jnp.dot(mixed, w_output, preferred_element_type=jnp.float32)
    attn_out = lax.psum(partial_out, "kvh")
    residual_full = (full_states.astype(jnp.float32) + attn_out).astype(jnp.bfloat16)
    residual_wide_full = residual_full.astype(jnp.float32)
    total_sq = jnp.sum(residual_wide_full * residual_wide_full, axis=-1, keepdims=True)
    residual_wide = lax.dynamic_slice_in_dim(
        residual_wide_full, kvh_index * width_local, width_local, axis=1
    )
    normed_two = (
        residual_wide * lax.rsqrt(total_sq / D + EPSILON) * ffn_gain.astype(jnp.float32)
    ).astype(jnp.bfloat16)
    fresh_flat = fresh.reshape(row_count, kv_local * channels)
    gathered = lax.all_gather(
        jnp.concatenate([normed_two, fresh_flat], axis=1), "req", axis=0, tiled=True
    )
    normed_all = gathered[:, :width_local]
    fresh_all = gathered[:, width_local:].reshape(total_rows, kv_local, channels)
    ffn_width = w_gate.shape[1]
    joined = jnp.concatenate([w_gate, w_up], axis=1)
    partial_both = jnp.dot(normed_all, joined, preferred_element_type=jnp.float32)
    summed = lax.psum(partial_both, "kvh")
    hidden = (jax.nn.silu(summed[:, :ffn_width]) * summed[:, ffn_width:]).astype(jnp.bfloat16)
    lowered = lax.psum_scatter(
        jnp.dot(hidden, w_down, preferred_element_type=jnp.float32),
        "req",
        scatter_dimension=0,
        tiled=True,
    )
    result = (residual_wide + lowered).astype(jnp.bfloat16)
    arrived = received[source_owner]
    new_blocks = mask_blocks(arrived, lengths[arriving], fresh_all[arriving])
    new_pool = new_blocks.reshape(row_count * pages_per, kv_local, page_len, channels)
    return (result, new_pool)


def solution(mesh):
    in_specs = (
        P("req", "kvh"),
        P(),
        P(None, "kvh"),
        P(None, "kvh"),
        P(None, "kvh"),
        P(),
        P(),
        P("kvh", None),
        P("kvh"),
        P("kvh", "req"),
        P("kvh", "req"),
        P("req", "kvh"),
        P("req", "kvh", None, None),
        P(),
        P("req", None),
        P(),
    )
    out_specs = (P("req", "kvh"), P("req", "kvh", None, None))
    return jax.shard_map(
        per_device, mesh=mesh, in_specs=in_specs, out_specs=out_specs, check_vma=False
    )
```

profile of v0, /device:TPU:0, one launch (start us, length us, event | category | flops | bytes accessed | tf_op | source)
XLA Modules:
  0.0 340.9 jit_solution(16654045882225741350)
XLA Ops:
  7.2 0.0 copy-start
  7.2 0.8 compare_select_fusion.4
  8.0 1.0 scatter_custom_fusion
  9.0 0.6 gather_fusion.3
  9.7 0.6 iota_reduce_fusion
  10.3 1.2 gather_fusion.4
  11.5 0.1 copy.35
  11.6 0.1 copy.36
  11.7 0.1 reshape.467
  11.8 8.7 %gather_fusion.5 = bf16[128,128,256]{2,1,0:T(8,128)(2,1)} fusion(bf16[64,128,256]{2,1,0:T(8,128)(2,1)} %bitcast.79, s32[1024]{0:T(1024)S(1)} %pad_clamp_fusion.1), kind=kCustom, calls=%fused_computation.5 | custom fusion | bytes 16777728 | tf_op jit(solution)/shard_map/gather | solution.py:106
  20.5 0.0 copy-start.5
  20.5 0.0 copy-start.4
  20.5 7.3 %all-to-all-start = ((bf16[16,8,1,128,256]{4,3,1,2,0:T(8,128)(2,1)}), bf16[16,8,1,128,256]{4,3,1,2,0:T(8,128)(2,1)}, u32[]{:S(2)}, u32[]{:S(2)}) async-start(bf16[16,8,1,128,256]{4,3,1,2,0:T(8,128)(2,1)} %bitcast.81), calls=%async_computation | async-start | bytes 16777216 | tf_op jit(solution)/shard_map/all_to_all | solution.py:107
  27.8 0.0 all-reduce.5.cloned.1.call-start
  27.9 0.0 copy-done.10
  27.9 0.6 gather_fusion
  28.6 0.1 reshape.433
  28.7 14.0 %all-gather = bf16[8,320,8]{1,2,0:T(8,128)(2,1)S(1)} all-gather(bf16[1,320,8]{1,2,0:T(8,128)(2,1)S(1)} %bitcast.84), channel_id=1, replica_groups=mesh['req'=16,'kvh'=8] {'kvh'}, dimensions={0}, use_global_device_ids=true | all-gather | bytes 46080 | tf_op jit(solution)/shard_map/all_gather | solution.py:110
  42.8 0.1 reshape.517
  42.9 0.1 fusion.18
  43.0 0.1 fusion.20
  43.1 2.3 multiply_reduce_fusion.1
  45.4 0.1 copy.33
  45.4 5.1 %gather_fusion.1 = bf16[64,128,256]{2,1,0:T(8,128)(2,1)} fusion(bf16[64,128,256]{2,1,0:T(8,128)(2,1)} %bitcast.80, s32[1024]{0:T(1024)S(1)} %pad_clamp_fusion.4), kind=kCustom, calls=%fused_computation.1 | custom fusion | bytes 8388864 | tf_op jit(solution)/shard_map/gather | solution.py:131
  50.6 0.2 fusion.9
  50.8 1.4 multiply_reduce_fusion.2
  52.2 0.1 multiply_bitcast_fusion
  52.3 0.1 fusion.37
  52.4 0.1 maximum_bitcast_fusion
  52.5 0.1 iota_add_fusion
  52.5 0.1 multiply_cosine_fusion.1
  52.7 0.1 broadcast_compare_fusion.1
  52.7 0.1 fusion.24
  52.8 0.1 subtract_convert_fusion
  52.9 7.6 %select_select_fusion.1 = bf16[8,1,1024,256]{3,2,0,1:T(8,128)(2,1)} fusion(bf16[8,1,1024,256]{3,2,0,1:T(8,128)(2,1)} %bitcast.83, pred[8,1024]{1,0:T(8,128)(4,1)S(1)} %get-tuple-element.13, pred[8,1024]{1,0:T(8,128)(4,1)S(1)} %get-tuple-element.12, bf16[8,256]{1,0:T(8,128)(2,1)S(1)} %maximum_bitcast_fusion), kind=kLoop, calls=%fused_computation.11 | loop fusion | flops 4194304 | bytes 8409088 | tf_op jit(solution)/shard_map/jit(_where)/select_n | solution.py:45
  60.6 2.5 fusion.48
  63.1 2.0 fusion.8
  65.1 1.1 fusion.26
  66.2 0.0 all-reduce.5.cloned.1.call-update
  66.2 0.0 all-reduce.7.cloned.1.call-start
  66.3 0.1 compare_select_fusion.9
  66.4 0.6 gather_fusion.2
  67.1 0.1 lt.107
  67.1 0.1 lt.108
  67.2 0.6 dynamic-slice
  68.5 56.2 %all-reduce.5.cloned.1.call-done = f32[8,2560]{1,0:T(8,128)} async-done(((f32[8,2560]{1,0:T(8,128)}), f32[8,2560]{1,0:T(8,128)}) %all-reduce.5.cloned.1.call-update) | async-done | bytes 81936 | tf_op jit(solution)/shard_map/psum | solution.py:137
  124.7 1.0 multiply_reduce_fusion
  125.7 0.1 multiply_convert_fusion
  125.8 0.1 pad_maximum_fusion
  125.9 41.0 %all_gather.7 = bf16[128,576]{1,0:T(8,128)(2,1)S(1)} all-gather(bf16[8,576]{1,0:T(8,128)(2,1)S(1)} %pad_maximum_fusion), channel_id=1, replica_groups=mesh['req'=16,'kvh'=8] {'req'}, dimensions={0}, use_global_device_ids=true | all-gather | bytes 156672 | tf_op jit(solution)/shard_map/all_gather | solution.py:148
  166.9 2.7 fusion.10
  169.6 0.0 all-reduce.7.cloned.1.call-update
  169.6 0.0 all-reduce.9.cloned.1.call-start
  169.7 0.1 bitcast_compare_fusion.1
  169.7 0.1 slice.63
  169.8 0.6 gather_fusion.7
  170.4 62.3 %all-reduce.7.cloned.1.call-done = f32[128,1216]{0,1:T(8,128)} async-done(((f32[128,1216]{0,1:T(8,128)}), f32[128,1216]{0,1:T(8,128)}) %all-reduce.7.cloned.1.call-update) | async-done | bytes 622608 | tf_op jit(solution)/shard_map/psum | solution.py:156
  232.8 2.2 fusion.15
  235.0 0.0 all-reduce.9.cloned.1.call-update
  235.0 84.2 %all-reduce.9.cloned.1.call-done = f32[128,320]{1,0:T(8,128)} async-done(((f32[128,320]{1,0:T(8,128)}), f32[128,320]{1,0:T(8,128)}) %all-reduce.9.cloned.1.call-update) | async-done | bytes 163856
  319.2 1.4 fusion.25
  320.5 0.0 all-to-all-done
  320.5 6.2 %gather_fusion.6 = bf16[8,8,128,256]{3,2,1,0:T(8,128)(2,1)} fusion(bf16[16,8,128,256]{3,2,1,0:T(8,128)(2,1)} %bitcast.16, s32[1024]{0:T(1024)S(1)} %pad_clamp_fusion), kind=kCustom, calls=%fused_computation.6 | custom fusion | bytes 8388640 | tf_op jit(solution)/shard_map/gather | solution.py:165
  326.7 7.6 %select_select_fusion = bf16[64,1,128,256]{3,2,1,0:T(8,128)(2,1)} fusion(bf16[64,1,128,256]{3,2,1,0:T(8,128)(2,1)} %bitcast.82, pred[64,128]{1,0:T(8,128)(4,1)S(1)} %get-tuple-element.11, pred[64,128]{1,0:T(8,128)(4,1)S(1)} %get-tuple-element.10, bf16[64,256]{1,0:T(8,128)(2,1)S(1)} %broadcast_bitcast_fusion), kind=kLoop, calls=%fused_computation.10 | loop fusion | flops 4194304 | bytes 8437760 | tf_op jit(solution)/shard_map/jit(_where)/select_n | solution.py:45
  (45 shorter events, 0.2 us)
Async XLA Ops:
  7.2 57.9 %copy-start = (bf16[512,2560]{1,0:T(8,128)(2,1)S(1)}, bf16[512,2560]{1,0:T(8,128)(2,1)}, u32[]{:S(2)}) copy-start(bf16[512,2560]{1,0:T(8,128)(2,1)} %param.23) | copy-start | bytes 7864324
  20.5 7.4 %copy-start.9 = (bf16[128]{0:T(256)(128)(2,1)S(1)}, bf16[128]{0:T(256)(128)(2,1)}, u32[]{:S(2)}) copy-start(bf16[128]{0:T(256)(128)(2,1)} %param.21) | copy-start | bytes 772
  20.5 7.5 %copy-start.10 = (bf16[128]{0:T(256)(128)(2,1)S(1)}, bf16[128]{0:T(256)(128)(2,1)}, u32[]{:S(2)}) copy-start(bf16[128]{0:T(256)(128)(2,1)} %param.22) | copy-start | bytes 772
  20.5 7.5 %copy-start.1 = (s32[128]{0:T(128)S(1)}, s32[128]{0:T(128)}, u32[]{:S(2)}) copy-start(s32[128]{0:T(128)} %param.29) | copy-start | bytes 1540
  20.5 8.1 %copy-start.2 = (s32[8,8]{1,0:T(8,128)S(1)}, s32[8,8]{1,0:T(8,128)}, u32[]{:S(2)}) copy-start(s32[8,8]{1,0:T(8,128)} %param.30) | copy-start | bytes 772
  20.5 8.2 %copy-start.5 = (bf16[2560]{0:T(1024)(128)(2,1)S(1)}, bf16[2560]{0:T(1024)(128)(2,1)}, u32[]{:S(2)}) copy-start(bf16[2560]{0:T(1024)(128)(2,1)} %param.17) | copy-start | bytes 15364
  20.5 8.2 %copy-start.4 = (bf16[8,320]{1,0:T(8,128)(2,1)S(1)}, bf16[8,320]{1,0:T(8,128)(2,1)}, u32[]{:S(2)}) copy-start(bf16[8,320]{1,0:T(8,128)(2,1)} %param.16) | copy-start | bytes 15364
  20.5 300.0 %all-to-all-start = ((bf16[16,8,1,128,256]{4,3,1,2,0:T(8,128)(2,1)}), bf16[16,8,1,128,256]{4,3,1,2,0:T(8,128)(2,1)}, u32[]{:S(2)}, u32[]{:S(2)}) async-start(bf16[16,8,1,128,256]{4,3,1,2,0:T(8,128)(2,1)} %bitcast.81), calls=%async_computation | async-start | bytes 16777216 | tf_op jit(solution)/shard_map/all_to_all | solution.py:107
  27.8 96.8 %all-reduce.5.cloned.1.call-start = ((), (), s32[]{:S(2)}) async-start(), calls=%async_computation.1 | async-start | bytes 163840 | tf_op jit(solution)/shard_map/psum | solution.py:137
  45.4 5.1 %copy-start.3 = (bf16[2560,128]{1,0:T(8,128)(2,1)S(1)}, bf16[2560,128]{1,0:T(8,128)(2,1)}, u32[]{:S(2)}) copy-start(bf16[2560,128]{1,0:T(8,128)(2,1)} %param.20) | copy-start | bytes 1966084
  60.5 5.7 %copy-start.7 = (s32[128]{0:T(128)S(1)}, s32[128]{0:T(128)}, u32[]{:S(2)}) copy-start(s32[128]{0:T(128)} %param.31) | copy-start | bytes 1540
  60.6 5.9 %copy-start.6 = (bf16[320]{0:T(512)(128)(2,1)S(1)}, bf16[320]{0:T(512)(128)(2,1)}, u32[]{:S(2)}) copy-start(bf16[320]{0:T(512)(128)(2,1)} %param.24) | copy-start | bytes 1924
  60.6 6.7 %copy-start.11 = (u32[128]{0:T(128)S(1)}, u32[128]{0:T(128)}, u32[]{:S(2)}) copy-start(u32[128]{0:T(128)} %constant.91) | copy-start | bytes 1540
  60.6 106.4 %copy-start.8 = (bf16[320,608]{1,0:T(8,128)(2,1)S(1)}, bf16[320,608]{1,0:T(8,128)(2,1)}, u32[]{:S(2)}) copy-start(bf16[320,608]{1,0:T(8,128)(2,1)} %param.26) | copy-start | bytes 1167364
  66.2 166.5 %all-reduce.7.cloned.1.call-start = ((), (), s32[]{:S(2)}) async-start(), calls=%async_computation.2 | async-start | bytes 1245184 | tf_op jit(solution)/shard_map/psum | solution.py:156
  169.6 149.6 %all-reduce.9.cloned.1.call-start = ((), (), s32[]{:S(2)}) async-start(), calls=%async_computation.3 | async-start | bytes 393216
Sparse Core Ops, SparseCore 0:
  66.4 58.2 all-reduce.4
  169.7 62.9 all-reduce.6
  236.5 82.5 all-reduce.8
where the time goes:
time: 342 us; the launch traced here: 341 us
  waiting for transfers between devices  203 us (59%)
  blocking collectives  55.1 us (16%)
  local copies, waits for them, and re-layouts  26.1 us (8%)
  other arithmetic  20.4 us (6%)
  between operations  14.7 us (4%)
  matrix products  14.3 us (4%)
  starting transfers between devices  7.46 us (2%)
    unnamed x4, waiting for transfers between devices  84.2 us
    psum x1, waiting for transfers between devices, per_device(): summed = lax.psum(partial_both, 'kvh')  62.3 us
    psum x1, waiting for transfers between devices, per_device(): attn_out = lax.psum(partial_out, 'kvh')  56.2 us
    all_gather x1, blocking collectives, per_device(): lax.all_gather(jnp.concatenate([normed_two, fresh_flat], axis=1), 'req',...  41 us
    select_n x2, other arithmetic, mask_blocks(): jnp.where(kept, blocks, jnp.where(placed, fresh[:, None, :, None, :], jnp...  15.3 us
    all_gather x1, blocking collectives, per_device(): full_states = lax.all_gather(states, 'kvh', axis=1, tiled=True)  14 us
    gather x3, local copies, waits for them, and re-layouts, per_device(): parcels = kv_pool[page_table[picked]]  9.99 us
    all_to_all x1, starting transfers between devices, per_device(): lax.all_to_all(parcels, 'req', split_axis=0, concat_axis=0, tiled=True)  7.34 us
  transfers between devices with their start and end apart: 4, of which 3 were waited for; matrix products, arithmetic and copies ran while one was open for 10% of the time, Pallas kernels for 0%

commit v1 on v0

--- a/solution.py
+++ b/solution.py
@@ -6,6 +6,27 @@
 
 D = 2560
 EPSILON = 1e-06
+
+
+def ring_gather(shard, axis, dim):
+    count, index, rows = (lax.axis_size(axis), lax.axis_index(axis), shard.shape[dim])
+    right = [(i, (i + 1) % count) for i in range(count)]
+    backward = [(i, (i - 1) % count) for i in range(count)]
+    out = jnp.zeros((*shard.shape[:dim], count * rows, *shard.shape[dim + 1 :]), shard.dtype)
+    out = lax.dynamic_update_slice_in_dim(out, shard, index * rows, axis=dim)
+    from_left = from_right = shard
+    half = count // 2
+    for step in range(1, half + 1):
+        from_left = lax.ppermute(from_left, axis, right)
+        out = lax.dynamic_update_slice_in_dim(
+            out, from_left, (index - step) % count * rows, axis=dim
+        )
+        if step < count - half:
+            from_right = lax.ppermute(from_right, axis, backward)
+            out = lax.dynamic_update_slice_in_dim(
+                out, from_right, (index + step) % count * rows, axis=dim
+            )
+    return out
 
 
 def rms_norm(values, norm_gain):
@@ -107,7 +128,7 @@
     received = lax.all_to_all(parcels, "req", split_axis=0, concat_axis=0, tiled=True)
     arriving = lax.dynamic_slice_in_dim(new_order, my_index * row_count, row_count)
     source_owner = arriving // row_count
-    full_states = lax.all_gather(states, "kvh", axis=1, tiled=True)
+    full_states = ring_gather(states, "kvh", 1)
     normed = rms_norm(full_states.astype(jnp.float32), attn_gain.astype(jnp.float32)).astype(
         jnp.bfloat16
     )

time: 342 us -> 342 us (level)
  blocking collectives: 55.1 us -> 37.6 us
  starting transfers between devices: 7.46 us -> 16.9 us
  waiting for transfers between devices: 203 us -> 208 us
    all_gather x1 -> x0, blocking collectives: 14 us -> none  [per_device(): full_states = lax.all_gather(states, 'kvh', axis=1, tiled=True)]
    ppermute x0 -> x7, starting transfers between devices: none -> 9.47 us  [the longest x3 9.46 us: ring_gather(): from_right = lax.ppermute(from_right, axis, backward)]
    ppermute x0 -> x7, waiting for transfers between devices: none -> 5.39 us  [the longest x4 5.38 us: ring_gather(): from_left = lax.ppermute(from_left, axis, right)]
  transfers between devices with their start and end apart: 4 -> 11, of which waited for: 3 -> 6; matrix products, arithmetic and copies ran while one was open for 10% -> 11% of each run, Pallas kernels for 0% -> 0%
where the time goes in v1:
time: 342 us; the launch traced here: 341 us
  waiting for transfers between devices  208 us (61%)
  blocking collectives  37.6 us (11%)
  local copies, waits for them, and re-layouts  28.4 us (8%)
  other arithmetic  20.4 us (6%)
  starting transfers between devices  16.9 us (5%)
  between operations  14.8 us (4%)
  matrix products  14.5 us (4%)
    unnamed x4, waiting for transfers between devices  84.2 us
    psum x1, waiting for transfers between devices, per_device(): summed = lax.psum(partial_both, 'kvh')  62.3 us
    psum x1, waiting for transfers between devices, per_device(): attn_out = lax.psum(partial_out, 'kvh')  56.4 us
    all_gather x1, blocking collectives, per_device(): lax.all_gather(jnp.concatenate([normed_two, fresh_flat], axis=1), 'req',...  37.6 us
    select_n x2, other arithmetic, mask_blocks(): jnp.where(kept, blocks, jnp.where(placed, fresh[:, None, :, None, :], jnp...  15.3 us
    gather x3, local copies, waits for them, and re-layouts, per_device(): parcels = kv_pool[page_table[picked]]  9.99 us
    ppermute x3, starting transfers between devices, ring_gather(): from_right = lax.ppermute(from_right, axis, backward)  9.46 us
    all_to_all x1, starting transfers between devices, per_device(): lax.all_to_all(parcels, 'req', split_axis=0, concat_axis=0, tiled=True)  7.34 us
  transfers between devices with their start and end apart: 11, of which 6 were waited for; matrix products, arithmetic and copies ran while one was open for 11% of the time, Pallas kernels for 0%

profile of v1, /device:TPU:0, one launch (start us, length us, event | category | flops | bytes accessed | tf_op | source)
XLA Modules:
  0.0 340.9 jit_solution(18242022822348772223)
XLA Ops:
  7.2 0.8 compare_select_fusion.4
  8.0 1.0 scatter_custom_fusion
  9.0 0.6 gather_fusion.3
  9.7 0.6 iota_reduce_fusion
  10.3 1.2 gather_fusion.4
  11.5 0.1 copy.31
  11.6 0.1 copy.32
  11.7 0.1 reshape.467
  11.8 8.7 %gather_fusion.5 = bf16[128,128,256]{2,1,0:T(8,128)(2,1)} fusion(bf16[64,128,256]{2,1,0:T(8,128)(2,1)} %bitcast.56, s32[1024]{0:T(1024)S(1)} %pad_clamp_fusion.1), kind=kCustom, calls=%fused_computation.5 | custom fusion | bytes 16777728 | tf_op jit(solution)/shard_map/gather | solution.py:127
  20.5 7.3 %all-to-all-start = ((bf16[16,8,1,128,256]{4,3,1,2,0:T(8,128)(2,1)}), bf16[16,8,1,128,256]{4,3,1,2,0:T(8,128)(2,1)}, u32[]{:S(2)}, u32[]{:S(2)}) async-start(bf16[16,8,1,128,256]{4,3,1,2,0:T(8,128)(2,1)} %bitcast.58), calls=%async_computation | async-start | bytes 16777216 | tf_op jit(solution)/shard_map/all_to_all | solution.py:128
  27.9 3.2 collective-permute-start.1
  31.1 0.6 gather_fusion
  31.8 0.1 iota_add_fusion
  31.9 0.1 multiply_cosine_fusion.1
  32.0 0.1 broadcast_compare_fusion.1
  32.1 0.1 reshape.433
  32.2 3.2 collective-permute-done
  35.4 3.0 collective-permute-start.3
  38.4 1.3 collective-permute-done.2
  39.7 0.1 compare_select_fusion.9
  39.8 3.3 collective-permute-start.5
  43.0 0.9 collective-permute-done.4
  44.0 5.1 %gather_fusion.1 = bf16[64,128,256]{2,1,0:T(8,128)(2,1)} fusion(bf16[64,128,256]{2,1,0:T(8,128)(2,1)} %bitcast.57, s32[1024]{0:T(1024)S(1)} %pad_clamp_fusion.4), kind=kCustom, calls=%fused_computation.1 | custom fusion | bytes 8388864 | tf_op jit(solution)/shard_map/gather | solution.py:152
  49.1 0.2 dynamic_update_slice.24
  49.3 0.3 dynamic_update_slice.25
  49.6 0.4 dynamic_update_slice.26
  50.0 0.3 dynamic_update_slice.27
  50.3 0.3 dynamic_update_slice.28
  50.5 0.4 dynamic_update_slice.29
  50.9 0.4 dynamic_update_slice.30
  51.3 0.3 dynamic_update_slice.31
  51.5 0.1 fusion.18
  51.7 2.3 multiply_reduce_fusion.1
  54.0 0.1 copy.29
  54.1 0.3 fusion.9
  54.4 1.5 multiply_reduce_fusion.2
  55.8 0.1 multiply_bitcast_fusion
  55.9 0.1 fusion.37
  56.0 0.1 maximum_bitcast_fusion
  56.1 0.1 fusion.24
  56.2 0.1 subtract_convert_fusion
  56.3 7.6 %select_select_fusion.1 = bf16[8,1,1024,256]{3,2,0,1:T(8,128)(2,1)} fusion(bf16[8,1,1024,256]{3,2,0,1:T(8,128)(2,1)} %bitcast.60, pred[8,1024]{1,0:T(8,128)(4,1)S(1)} %get-tuple-element.13, pred[8,1024]{1,0:T(8,128)(4,1)S(1)} %get-tuple-element.12, bf16[8,256]{1,0:T(8,128)(2,1)S(1)} %maximum_bitcast_fusion), kind=kLoop, calls=%fused_computation.11 | loop fusion | flops 4194304 | bytes 8409088 | tf_op jit(solution)/shard_map/jit(_where)/select_n | solution.py:66
  63.9 2.5 fusion.52
  66.4 2.0 fusion.8
  68.5 1.1 fusion.26
  69.7 0.6 gather_fusion.2
  70.3 0.1 lt.173
  70.4 0.1 lt.174
  70.5 0.6 dynamic-slice
  71.7 56.4 %all-reduce.5.cloned.1.call-done = f32[8,2560]{1,0:T(8,128)} async-done(((f32[8,2560]{1,0:T(8,128)}), f32[8,2560]{1,0:T(8,128)}) %all-reduce.5.cloned.1.call-update) | async-done | bytes 81936 | tf_op jit(solution)/shard_map/psum | solution.py:158
  128.1 1.0 multiply_reduce_fusion
  129.1 0.1 multiply_convert_fusion
  129.2 0.1 pad_maximum_fusion
  129.3 37.6 %all_gather.3 = bf16[128,576]{1,0:T(8,128)(2,1)S(1)} all-gather(bf16[8,576]{1,0:T(8,128)(2,1)S(1)} %pad_maximum_fusion), channel_id=1, replica_groups=mesh['req'=16,'kvh'=8] {'req'}, dimensions={0}, use_global_device_ids=true | all-gather | bytes 156672 | tf_op jit(solution)/shard_map/all_gather | solution.py:169
  166.9 2.7 fusion.10
  169.7 0.1 bitcast_compare_fusion.1
  169.8 0.1 slice.63
  169.9 0.6 gather_fusion.7
  170.4 62.3 %all-reduce.7.cloned.1.call-done = f32[128,1216]{0,1:T(8,128)} async-done(((f32[128,1216]{0,1:T(8,128)}), f32[128,1216]{0,1:T(8,128)}) %all-reduce.7.cloned.1.call-update) | async-done | bytes 622608 | tf_op jit(solution)/shard_map/psum | solution.py:177
  232.8 2.2 fusion.15
  235.0 84.2 %all-reduce.9.cloned.1.call-done = f32[128,320]{1,0:T(8,128)} async-done(((f32[128,320]{1,0:T(8,128)}), f32[128,320]{1,0:T(8,128)}) %all-reduce.9.cloned.1.call-update) | async-done | bytes 163856
  319.2 1.4 fusion.25
  320.5 6.2 %gather_fusion.6 = bf16[8,8,128,256]{3,2,1,0:T(8,128)(2,1)} fusion(bf16[16,8,128,256]{3,2,1,0:T(8,128)(2,1)} %bitcast.13, s32[1024]{0:T(1024)S(1)} %pad_clamp_fusion), kind=kCustom, calls=%fused_computation.6 | custom fusion | bytes 8388640 | tf_op jit(solution)/shard_map/gather | solution.py:186
  326.8 7.6 %select_select_fusion = bf16[64,1,128,256]{3,2,1,0:T(8,128)(2,1)} fusion(bf16[64,1,128,256]{3,2,1,0:T(8,128)(2,1)} %bitcast.59, pred[64,128]{1,0:T(8,128)(4,1)S(1)} %get-tuple-element.11, pred[64,128]{1,0:T(8,128)(4,1)S(1)} %get-tuple-element.10, bf16[64,256]{1,0:T(8,128)(2,1)S(1)} %broadcast_bitcast_fusion), kind=kLoop, calls=%fused_computation.10 | loop fusion | flops 4194304 | bytes 8437760 | tf_op jit(solution)/shard_map/jit(_where)/select_n | solution.py:66
  (64 shorter events, 0.4 us)
Async XLA Ops:
  7.2 61.3 %copy-start = (bf16[512,2560]{1,0:T(8,128)(2,1)S(1)}, bf16[512,2560]{1,0:T(8,128)(2,1)}, u32[]{:S(2)}) copy-start(bf16[512,2560]{1,0:T(8,128)(2,1)} %param.23) | copy-start | bytes 7864324
  20.5 7.4 %copy-start.5 = (bf16[8,320]{1,0:T(8,128)(2,1)S(1)}, bf16[8,320]{1,0:T(8,128)(2,1)}, u32[]{:S(2)}) copy-start(bf16[8,320]{1,0:T(8,128)(2,1)} %param.16) | copy-start | bytes 15364
  20.5 10.7 %copy-start.1 = (s32[128]{0:T(128)S(1)}, s32[128]{0:T(128)}, u32[]{:S(2)}) copy-start(s32[128]{0:T(128)} %param.29) | copy-start | bytes 1540
  20.5 11.6 %copy-start.2 = (s32[8,8]{1,0:T(8,128)S(1)}, s32[8,8]{1,0:T(8,128)}, u32[]{:S(2)}) copy-start(s32[8,8]{1,0:T(8,128)} %param.30) | copy-start | bytes 772
  20.5 19.2 %copy-start.7 = (s32[128]{0:T(128)S(1)}, s32[128]{0:T(128)}, u32[]{:S(2)}) copy-start(s32[128]{0:T(128)} %param.31) | copy-start | bytes 1540
  20.5 23.5 %copy-start.9 = (bf16[128]{0:T(256)(128)(2,1)S(1)}, bf16[128]{0:T(256)(128)(2,1)}, u32[]{:S(2)}) copy-start(bf16[128]{0:T(256)(128)(2,1)} %param.21) | copy-start | bytes 772
  20.5 23.5 %copy-start.10 = (bf16[128]{0:T(256)(128)(2,1)S(1)}, bf16[128]{0:T(256)(128)(2,1)}, u32[]{:S(2)}) copy-start(bf16[128]{0:T(256)(128)(2,1)} %param.22) | copy-start | bytes 772
  20.5 23.5 %copy-start.4 = (bf16[2560]{0:T(1024)(128)(2,1)S(1)}, bf16[2560]{0:T(1024)(128)(2,1)}, u32[]{:S(2)}) copy-start(bf16[2560]{0:T(1024)(128)(2,1)} %param.17) | copy-start | bytes 15364
  20.5 300.0 %all-to-all-start = ((bf16[16,8,1,128,256]{4,3,1,2,0:T(8,128)(2,1)}), bf16[16,8,1,128,256]{4,3,1,2,0:T(8,128)(2,1)}, u32[]{:S(2)}, u32[]{:S(2)}) async-start(bf16[16,8,1,128,256]{4,3,1,2,0:T(8,128)(2,1)} %bitcast.58), calls=%async_computation | async-start | bytes 16777216 | tf_op jit(solution)/shard_map/all_to_all | solution.py:128
  27.9 100.2 %all-reduce.5.cloned.1.call-start = ((), (), s32[]{:S(2)}) async-start(), calls=%async_computation.1 | async-start | bytes 163840 | tf_op jit(solution)/shard_map/psum | solution.py:158
  27.9 7.5 %collective-permute-start.1 = (bf16[8,320]{1,0:T(8,128)(2,1)S(1)}, bf16[8,320]{1,0:T(8,128)(2,1)S(1)}, u32[]{:S(2)}, u32[]{:S(2)}) collective-permute-start(bf16[8,320]{1,0:T(8,128)(2,1)S(1)} %copy-done.5), channel_id=1, source_target_pairs={{0,7},{1,0},{2,1},{3,2},{4,3},{5,4},{6,5},{7,6},{8,15},{9,8},{10,9... | collective-permute-start | bytes 15368 | tf_op jit(solution)/shard_map/ppermute | solution.py:25
  31.1 4.3 %collective-permute-start = (bf16[8,320]{1,0:T(8,128)(2,1)S(1)}, bf16[8,320]{1,0:T(8,128)(2,1)S(1)}, u32[]{:S(2)}, u32[]{:S(2)}) collective-permute-start(bf16[8,320]{1,0:T(8,128)(2,1)S(1)} %copy-done.5), channel_id=1, source_target_pairs={{0,1},{1,2},{2,3},{3,4},{4,5},{5,6},{6,7},{7,0},{8,9},{9,10},{10,1... | collective-permute-start | bytes 15368 | tf_op jit(solution)/shard_map/ppermute | solution.py:20
  35.4 4.3 %collective-permute-start.2 = (bf16[8,320]{1,0:T(8,128)(2,1)S(1)}, bf16[8,320]{1,0:T(8,128)(2,1)S(1)}, u32[]{:S(2)}, u32[]{:S(2)}) collective-permute-start(bf16[8,320]{1,0:T(8,128)(2,1)S(1)} %collective-permute-done), channel_id=1, source_target_pairs={{0,1},{1,2},{2,3},{3,4},{4,5},{5,6},{6,7},{7,0},{8,9},{9,10},{10,1... | collective-permute-start | bytes 15368 | tf_op jit(solution)/shard_map/ppermute | solution.py:20
  35.4 4.3 %collective-permute-start.3 = (bf16[8,320]{1,0:T(8,128)(2,1)S(1)}, bf16[8,320]{1,0:T(8,128)(2,1)S(1)}, u32[]{:S(2)}, u32[]{:S(2)}) collective-permute-start(bf16[8,320]{1,0:T(8,128)(2,1)S(1)} %collective-permute-done.1), channel_id=1, source_target_pairs={{0,7},{1,0},{2,1},{3,2},{4,3},{5,4},{6,5},{7,6},{8,15},{9,8},{10,9... | collective-permute-start | bytes 15368 | tf_op jit(solution)/shard_map/ppermute | solution.py:25
  39.7 4.3 %collective-permute-start.4 = (bf16[8,320]{1,0:T(8,128)(2,1)S(1)}, bf16[8,320]{1,0:T(8,128)(2,1)S(1)}, u32[]{:S(2)}, u32[]{:S(2)}) collective-permute-start(bf16[8,320]{1,0:T(8,128)(2,1)S(1)} %collective-permute-done.2), channel_id=1, source_target_pairs={{0,1},{1,2},{2,3},{3,4},{4,5},{5,6},{6,7},{7,0},{8,9},{9,10},{10,1... | collective-permute-start | bytes 15368 | tf_op jit(solution)/shard_map/ppermute | solution.py:20
  39.8 11.1 %collective-permute-start.5 = (bf16[8,320]{1,0:T(8,128)(2,1)S(1)}, bf16[8,320]{1,0:T(8,128)(2,1)S(1)}, u32[]{:S(2)}, u32[]{:S(2)}) collective-permute-start(bf16[8,320]{1,0:T(8,128)(2,1)S(1)} %collective-permute-done.3), channel_id=1, source_target_pairs={{0,7},{1,0},{2,1},{3,2},{4,3},{5,4},{6,5},{7,6},{8,15},{9,8},{10,9... | collective-permute-start | bytes 15368 | tf_op jit(solution)/shard_map/ppermute | solution.py:25
  43.9 7.3 %collective-permute-start.6 = (bf16[8,320]{1,0:T(8,128)(2,1)S(1)}, bf16[8,320]{1,0:T(8,128)(2,1)S(1)}, u32[]{:S(2)}, u32[]{:S(2)}) collective-permute-start(bf16[8,320]{1,0:T(8,128)(2,1)S(1)} %collective-permute-done.4), channel_id=1, source_target_pairs={{0,1},{1,2},{2,3},{3,4},{4,5},{5,6},{6,7},{7,0},{8,9},{9,10},{10,1... | collective-permute-start | bytes 15368 | tf_op jit(solution)/shard_map/ppermute | solution.py:20
  44.0 10.1 %copy-start.3 = (bf16[2560,128]{1,0:T(8,128)(2,1)S(1)}, bf16[2560,128]{1,0:T(8,128)(2,1)}, u32[]{:S(2)}) copy-start(bf16[2560,128]{1,0:T(8,128)(2,1)} %param.20) | copy-start | bytes 1966084
  63.9 5.7 %copy-start.6 = (bf16[320]{0:T(512)(128)(2,1)S(1)}, bf16[320]{0:T(512)(128)(2,1)}, u32[]{:S(2)}) copy-start(bf16[320]{0:T(512)(128)(2,1)} %param.24) | copy-start | bytes 1924
  63.9 6.6 %copy-start.11 = (u32[128]{0:T(128)S(1)}, u32[128]{0:T(128)}, u32[]{:S(2)}) copy-start(u32[128]{0:T(128)} %constant.137) | copy-start | bytes 1540
  63.9 103.0 %copy-start.8 = (bf16[320,608]{1,0:T(8,128)(2,1)S(1)}, bf16[320,608]{1,0:T(8,128)(2,1)}, u32[]{:S(2)}) copy-start(bf16[320,608]{1,0:T(8,128)(2,1)} %param.26) | copy-start | bytes 1167364
  69.6 163.2 %all-reduce.7.cloned.1.call-start = ((), (), s32[]{:S(2)}) async-start(), calls=%async_computation.2 | async-start | bytes 1245184 | tf_op jit(solution)/shard_map/psum | solution.py:177
  169.6 149.6 %all-reduce.9.cloned.1.call-start = ((), (), s32[]{:S(2)}) async-start(), calls=%async_computation.3 | async-start | bytes 393216
Sparse Core Ops, SparseCore 0:
  69.7 58.3 all-reduce.4
  169.7 62.9 all-reduce.6
  236.6 82.5 all-reduce.8
